TPU v7x, 256 devices: a whole 4x4x8 slice. The times are simulated.
256 devices in a mesh: grp: 32 (over z, y_hi, core), tp: 8 (over y_lo, x).
Axes of the slice: x: 4, y: 4 (y_hi: 2, y_lo: 2; y = y_hi * 2 + y_lo), z: 8, core: 2. Of those that a mesh axis runs over, the one named last changes fastest.
Arguments:
- states_in: bfloat16 [16384, 1536], P('grp', 'tp'), may hold values from -6 to 6
- segment_ids: int32 [16384], P('grp'), may hold values from 0 to 223, as said below
- positions: int32 [16384], P('grp'), may hold values from 0 to 1009, as said below
- attention_gain: bfloat16 [1536], P('tp'), may hold values from 0.5 to 1.5
- feedforward_gain: bfloat16 [1536], P('tp'), may hold values from 0.5 to 1.5
- query_weight: bfloat16 [1536, 1536], P('grp', 'tp'), may hold values from -1 to 1
- keyvalue_weight: bfloat16 [1536, 8, 128], P('grp', 'tp'), may hold values from -128 to 128
- output_weight: bfloat16 [1536, 1536], P('tp'), may hold values from -0.15625 to 0.15625
- route_experts: int32 [16384, 8], P('grp'), may hold values from 0 to 19, all different within a row; in each aligned block of 512 rows (0 to 511, 512 to 1023, ...) at most 256 rows name the same one
- route_weights: float32 [16384, 8], P('grp'), may hold values from 0.05 to 0.3
- expert_gateup: bfloat16 [40, 1536, 512], P('tp'), may hold values from -0.15625 to 0.15625
- expert_down: bfloat16 [40, 256, 1536], P('tp'), may hold values from -0.25 to 0.25
- cache_slots: int32 [16384], P('grp'), may hold values from 0 to 16383, as said below
Outputs:
- layer_output: bfloat16 [16384, 1536], P('grp', 'tp')
- paged_cache: bfloat16 [16384, 8, 128], P('grp', 'tp')
- log_sums: float32 [24, 16384], P('tp', 'grp')
Inputs may be any that keep to these rules, and one draw needn't show every extreme that they name: `segment_ids`: equal ids mark the tokens of one prompt; the tokens of a prompt lie within one pair of groups 2p and 2p+1. `positions`: positions count from 0 within each prompt; one prompt of groups 0 and 1 has 2 * (505) tokens. `route_experts`: each row names 8 different experts; at most 256 rows of one group name the same expert, and that number is reached. `cache_slots`: every cache row is named once; the tokens of each group fill exactly 16 rows of every group's block of 512 rows.
All inputs are finite; a program needn't handle non-finite values.
Results may differ from a plain program's by a relative error of at most 0.01.
The roundings to bfloat16 on the way count: a program that leaves them out, or rounds other values in their place, can miss the bound.
Values may be sent and summed in bfloat16 or wider, within the bound.
No kernel may reach another device: no remote copies, remote signals or barrier semaphores. Data moves between devices by JAX's collectives and lax.ppermute only.
A program may use at most 128 MiB of HBM per device.

v0:
```python
import jax
import jax.numpy as jnp
from jax import lax
from jax.sharding import Mesh
from jax.sharding import PartitionSpec as P

HD = 64
attn_scale = 0.015625
norm_eps = 1e-06
rope_base = 10000.0
G = ("z", "yh", "c")
T = ("yl", "x")


def rms_scale(values, gain_row):
    floats = values.astype(jnp.float32)
    mean_square = jnp.mean(floats * floats, axis=-1, keepdims=True)
    return (floats * lax.rsqrt(mean_square + norm_eps) * gain_row.astype(jnp.float32)).astype(
        jnp.bfloat16
    )


def rotate(values, places):
    half_width = values.shape[-1] // 2
    frequency = rope_base ** (-jnp.arange(half_width, dtype=jnp.float32) * 2.0 / values.shape[-1])
    angles = places.astype(jnp.float32)[:, None] * frequency[None, :]
    cosine = jnp.cos(angles)[:, None, :]
    sine_part = jnp.sin(angles)[:, None, :]
    leading = values[..., :half_width]
    trailing = values[..., half_width:]
    return jnp.concatenate(
        [leading * cosine - trailing * sine_part, trailing * cosine + leading * sine_part], axis=-1
    )


def attend_block(query_block, seg_block, pos_block, all_rows, all_seg, all_pos):
    key_part = all_rows[..., :HD]
    value_part = all_rows[..., HD:]
    scores = (
        jnp.einsum("qgrd,kgd->grqk", query_block, key_part, preferred_element_type=jnp.float32)
        * attn_scale
    )
    allowed = (seg_block[:, None] == all_seg[None, :]) & (all_pos[None, :] <= pos_block[:, None])
    masked = jnp.where(allowed, scores, -jnp.inf)
    row_peak = jnp.max(masked, axis=-1, keepdims=True)
    exponent = jnp.exp(masked - row_peak)
    row_total = jnp.sum(exponent, axis=-1, keepdims=True)
    log_total = (row_peak + jnp.log(row_total))[..., 0]
    weights_low = (exponent / row_total).astype(jnp.bfloat16)
    mixed_rows = jnp.einsum(
        "grqk,kgd->qgrd", weights_low, value_part, preferred_element_type=jnp.float32
    )
    return (mixed_rows.astype(jnp.bfloat16), log_total)


def expert_terms(normed, route_experts, route_weights, gateup, down, slot_first):
    local_experts = gateup.shape[0]
    half_units = down.shape[1]
    owned_experts = slot_first + jnp.arange(local_experts, dtype=jnp.int32)
    matches = route_experts[:, :, None] == owned_experts[None, None, :]
    route_scale = jnp.sum(jnp.where(matches, route_weights[:, :, None], 0.0), axis=1)
    gate_up = jnp.einsum("td,edf->etf", normed, gateup, preferred_element_type=jnp.float32)
    activated = (jax.nn.silu(gate_up[..., :half_units]) * gate_up[..., half_units:]).astype(
        jnp.bfloat16
    )
    produced = jnp.einsum("etf,efd->etd", activated, down, preferred_element_type=jnp.float32)
    return jnp.sum(route_scale.T[:, :, None] * produced, axis=0)


def gather_rows_over_groups(block):
    width = block.shape[1]
    nz = lax.axis_size("z")
    zi = lax.axis_index("z")
    got = [block]
    for k in range(1, nz):
        got.append(lax.ppermute(block, "z", [(i, (i + k) % nz) for i in range(nz)]))
    stacked = jnp.stack(got)
    zfull = jnp.take(stacked, (zi - jnp.arange(nz)) % nz, axis=0)
    yi = lax.axis_index("yh")
    other_y = lax.ppermute(zfull, "yh", [(0, 1), (1, 0)])
    yfull = jnp.where(yi == 0, jnp.stack([zfull, other_y]), jnp.stack([other_y, zfull]))
    ci = lax.axis_index("c")
    other_c = lax.ppermute(yfull, "c", [(0, 1), (1, 0)])
    cfull = jnp.where(ci == 0, jnp.stack([yfull, other_c]), jnp.stack([other_c, yfull]))
    return cfull.transpose(2, 1, 0, 3, 4).reshape(-1, width)


def shards(
    states_in,
    segment_ids,
    positions,
    attention_gain,
    feedforward_gain,
    query_weight,
    keyvalue_weight,
    output_weight,
    route_experts,
    route_weights,
    expert_gateup,
    expert_down,
    cache_slots,
):
    tokens = states_in.shape[0]
    width_share = states_in.shape[1]
    head_rank = lax.axis_index(T)
    group_rank = lax.axis_index(G)
    gain_rows = jnp.zeros((8, width_share), states_in.dtype)
    gain_rows = gain_rows.at[0].set(attention_gain).at[1].set(feedforward_gain)
    packed = jnp.concatenate([states_in, gain_rows], axis=0)
    packed_full = lax.all_gather(packed, T, axis=1, tiled=True)
    states_full = packed_full[:tokens]
    gain_attend = packed_full[tokens]
    gain_forward = packed_full[tokens + 1]
    normed_in = rms_scale(states_full, gain_attend)
    query_cols = query_weight.shape[1]
    keyvalue_heads = keyvalue_weight.shape[1]
    heads_local = query_cols // HD
    piece_rows = query_weight.shape[0]
    weights_packed = jnp.concatenate(
        [query_weight, keyvalue_weight.reshape(piece_rows, -1)], axis=1
    )
    weights_full = gather_rows_over_groups(weights_packed)
    query_full_w = weights_full[:, :query_cols]
    keyvalue_full_w = weights_full[:, query_cols:]
    query_sum = jnp.dot(normed_in, query_full_w, preferred_element_type=jnp.float32)
    keyvalue_sum = jnp.dot(normed_in, keyvalue_full_w, preferred_element_type=jnp.float32)
    queries = rotate(query_sum.reshape(tokens, heads_local, HD), positions).astype(jnp.bfloat16)
    keyvalue_sum = keyvalue_sum.reshape(tokens, keyvalue_heads, 2 * HD)
    key_rows = rotate(keyvalue_sum[..., :HD], positions).astype(jnp.bfloat16)
    value_rows = keyvalue_sum[..., HD:].astype(jnp.bfloat16)
    own_rows = jnp.concatenate([key_rows, value_rows], axis=-1)
    other_rows, other_seg, other_pos = lax.ppermute(
        (own_rows, segment_ids, positions), "c", [(0, 1), (1, 0)]
    )
    all_rows = jnp.concatenate([own_rows, other_rows], axis=0)
    all_seg = jnp.concatenate([segment_ids, other_seg], axis=0)
    all_pos = jnp.concatenate([positions, other_pos], axis=0)
    group_ratio = heads_local // keyvalue_heads
    query_block = queries.reshape(tokens, keyvalue_heads, group_ratio, HD)
    mixed, log_part = attend_block(query_block, segment_ids, positions, all_rows, all_seg, all_pos)
    attended = mixed.reshape(tokens, heads_local * HD)
    log_sums = log_part.reshape(heads_local, tokens)
    partial_value = jnp.dot(attended, output_weight, preferred_element_type=jnp.float32)
    summed = lax.psum(partial_value, T)
    residual = (states_full.astype(jnp.float32) + summed).astype(jnp.bfloat16)
    normed = rms_scale(residual, gain_forward)
    residual_share = lax.dynamic_slice_in_dim(residual, head_rank * width_share, width_share, 1)
    slot_first = head_rank // 2 * expert_gateup.shape[0]
    terms = expert_terms(
        normed, route_experts, route_weights, expert_gateup, expert_down, slot_first
    )
    expert_share = lax.psum_scatter(
        terms.astype(jnp.bfloat16), T, scatter_dimension=1, tiled=True
    ).astype(jnp.float32)
    layer_output = (residual_share.astype(jnp.float32) + expert_share).astype(jnp.bfloat16)
    group_count = lax.axis_size(G)
    per_owner = tokens // group_count
    owners = cache_slots // tokens
    sequence = jnp.arange(tokens, dtype=jnp.int32)
    ordering = jnp.argsort(owners * tokens + sequence)
    send_rows = own_rows[ordering].reshape(group_count, per_owner, keyvalue_heads, 2 * HD)
    send_slots = cache_slots[ordering].reshape(group_count, per_owner)
    got_rows, got_slots = (
        lax.all_to_all(send_rows, G, split_axis=0, concat_axis=0, tiled=True),
        lax.all_to_all(send_slots, G, split_axis=0, concat_axis=0, tiled=True),
    )
    targets = got_slots.reshape(tokens) - group_rank * tokens
    paged_rows = (
        jnp.zeros_like(own_rows).at[targets].set(got_rows.reshape(tokens, keyvalue_heads, 2 * HD))
    )
    return (layer_output, paged_rows, log_sums)


def solution(mesh):
    fine = Mesh(mesh.devices.reshape(8, 2, 2, 2, 4), ("z", "yh", "c", "yl", "x"))
    return jax.shard_map(
        shards,
        mesh=fine,
        in_specs=(
            P(G, T),
            P(G),
            P(G),
            P(T),
            P(T),
            P(G, T),
            P(G, T, None),
            P(T, None),
            P(G, None),
            P(G, None),
            P(T, None, None),
            P(T, None, None),
            P(G),
        ),
        out_specs=(P(G, T), P(G, T, None), P(T, G)),
        check_vma=False,
    )
```

profile of v0, /device:TPU:1, one launch (start us, length us, event | category | flops | bytes accessed | tf_op | source)
XLA Modules:
  0.0 252.0 jit_solution(752531297667724004)
XLA Ops:
  7.2 0.9 pad_maximum_fusion.3
  8.1 2.5 collective-permute-start
  10.6 3.0 %collective-permute-start.1 = (bf16[48,320]{1,0:T(8,128)(2,1)S(1)}, bf16[48,320]{1,0:T(8,128)(2,1)S(1)}, u32[]{:S(2)}, u32[]{:S(2)}) collective-permute-start(bf16[48,320]{1,0:T(8,128)(2,1)S(1)} %pad_maximum_fusion.3), channel_id=1, source_target_pairs={{0,64},{32,96},{64,128},{96,160},{128,192},{160,224},{192,0},{224,... | collective-permute-start | bytes 92168 | tf_op jit(solution)/shard_map/ppermute | solution.py:76
  13.6 3.8 %collective-permute-start.2 = (bf16[48,320]{1,0:T(8,128)(2,1)S(1)}, bf16[48,320]{1,0:T(8,128)(2,1)S(1)}, u32[]{:S(2)}, u32[]{:S(2)}) collective-permute-start(bf16[48,320]{1,0:T(8,128)(2,1)S(1)} %pad_maximum_fusion.3), channel_id=1, source_target_pairs={{0,96},{32,128},{64,160},{96,192},{128,224},{160,0},{192,32},{224,... | collective-permute-start | bytes 92168 | tf_op jit(solution)/shard_map/ppermute | solution.py:76
  17.8 0.7 reshape.415
  19.3 1.7 pad_maximum_fusion.1
  21.1 1.7 collective-permute-start.10
  22.7 0.8 bitcast_dynamic-update-slice_fusion.7
  23.6 0.7 convert_element_type.66
  24.7 4.7 %collective-permute-start.4 = (bf16[48,320]{1,0:T(8,128)(2,1)S(1)}, bf16[48,320]{1,0:T(8,128)(2,1)S(1)}, u32[]{:S(2)}, u32[]{:S(2)}) collective-permute-start(bf16[48,320]{1,0:T(8,128)(2,1)S(1)} %pad_maximum_fusion.3), channel_id=1, source_target_pairs={{0,160},{32,192},{64,224},{96,0},{128,32},{160,64},{192,96},{224,1... | collective-permute-start | bytes 92168 | tf_op jit(solution)/shard_map/ppermute | solution.py:76
  29.4 0.7 pad_add_fusion
  30.1 2.5 collective-permute-start.5
  32.6 0.8 collective-permute-start.6
  33.4 0.9 collective-permute-start.11
  34.6 0.8 collective-permute-done.6
  36.2 3.0 %collective-permute-start.7 = (bf16[8,48,320]{2,1,0:T(8,128)(2,1)S(1)}, bf16[8,48,320]{2,1,0:T(8,128)(2,1)S(1)}, u32[]{:S(2)}, u32[]{:S(2)}) collective-permute-start(bf16[8,48,320]{2,1,0:T(8,128)(2,1)S(1)} %broadcast_select_fusion), channel_id=1, source_target_pairs={{0,16},{16,0},{1,17},{17,1},{2,18},{18,2},{3,19},{19,3},{4,20},{20... | collective-permute-start | bytes 737288 | tf_op jit(solution)/shard_map/ppermute | solution.py:80
  39.2 0.7 pad_add_fusion.1
  40.0 23.9 %collective-permute-done.7 = bf16[8,48,320]{2,1,0:T(8,128)(2,1)S(1)} collective-permute-done((bf16[8,48,320]{2,1,0:T(8,128)(2,1)S(1)}, bf16[8,48,320]{2,1,0:T(8,128)(2,1)S(1)}, u32[]{:S(2)}, u32[]{:S(2)}) %collective-permute-start.7) | collective-permute-done | bytes 245792 | tf_op jit(solution)/shard_map/ppermute | solution.py:80
  64.1 0.8 collective-permute-start.8
  64.8 0.8 compare_and_fusion
  66.8 1.1 copy.50
  68.0 2.6 %slice.95 = bf16[512,1536]{0,1:T(8,128)(2,1)} slice(bf16[520,1536]{0,1:T(8,128)(2,1)} %all-gather.2.cloned.1.call-done), slice={[0:512], [0:1536]} | slice | bytes 3145728 | tf_op jit(solution)/shard_map/slice | solution.py:111
  70.6 1.7 copy.59
  72.7 1.5 convert_reduce_fusion
  74.3 2.0 convolution_bitcast_fusion.1
  76.6 0.8 fusion.22
  78.0 0.9 collective-permute-done.9
  78.9 1.3 fusion.1
  80.2 1.4 fusion
  81.6 2.0 fusion.19
  83.7 2.3 fusion.54
  86.5 91.7 %all-reduce.3.cloned.1.call-done = f32[512,1536]{1,0:T(8,128)} async-done(((f32[512,1536]{1,0:T(8,128)}), f32[512,1536]{1,0:T(8,128)}) %all-reduce.3.cloned.1.call-update) | async-done | bytes 3145744 | tf_op jit(solution)/shard_map/psum | solution.py:144
  178.2 2.4 fusion.2
  180.6 7.5 %convolution_bitcast_fusion = f32[5,512,512]{2,1,0:T(8,128)S(1)} fusion(bf16[5,1536,512]{2,1,0:T(8,128)(2,1)} %param.27, bf16[512,1536]{1,0:T(8,128)(2,1)S(1)} %get-tuple-element.47, f32[1536]{0:T(1024)S(1)} %get-tuple-element.44, f32[512]{0:T(512)S(1)} %add_rsqrt_fusion), kind=kOutput, calls=%fused_computation.26 | convolution fusion | flops 4029677568 | bytes 14688256 | tf_op jit(solution)/shard_map/td,edf->etf/dot_general | solution.py:62
  188.2 3.5 %multiply_reduce_fusion = bf16[512,1536]{1,0:T(8,128)(2,1)S(1)} fusion(bf16[5,256,1536]{2,1,0:T(8,128)(2,1)S(1)} %copy-done.8, f32[5,512]{1,0:T(8,128)S(1)} %bitcast.103, f32[5,512,512]{2,1,0:T(8,128)S(1)} %convolution_bitcast_fusion), kind=kOutput, calls=%fused_computation.4 | convolution fusion | flops 2024275968 | bytes 10758144 | tf_op jit(solution)/shard_map/etf,efd->etd/dot_general | solution.py:66
  191.7 1.6 copy.57
  193.3 3.8 %sort.17 = (s32[512]{0:T(512)}, s32[512]{0:T(512)S(1)}) sort(s32[512]{0:T(512)S(1)} %fusion.43, s32[512]{0:T(512)S(1)} %iota.31), dimensions={0}, to_apply=%region_8.9 | sort | flops 4608 | bytes 8192 | tf_op jit(solution)/shard_map/jit(argsort)/sort | solution.py:160
  197.1 3.5 %gather_fusion.1 = s32[512]{0:T(512)S(1)} fusion(s32[512]{0:T(512)S(1)} %copy-done.1, s32[1024]{0:T(1024)S(1)} %pad_clamp_fusion), kind=kCustom, calls=%fused_computation.1 | custom fusion | bytes 6144 | tf_op jit(solution)/shard_map/gather | solution.py:162
  200.6 0.7 all_to_all.9
  201.3 12.2 %all-to-all-start = ((s32[32,1,16]{2,1,0:T(1,128)}), s32[32,1,16]{2,1,0:T(1,128)S(1)}, u32[]{:S(2)}, u32[]{:S(2)}) async-start(s32[32,1,16]{2,1,0:T(1,128)} %bitcast.32), calls=%async_computation | async-start | bytes 32768 | tf_op jit(solution)/shard_map/all_to_all | solution.py:165
  213.5 9.3 %all-to-all-done = s32[32,1,16]{2,1,0:T(1,128)S(1)} async-done(((s32[32,1,16]{2,1,0:T(1,128)}), s32[32,1,16]{2,1,0:T(1,128)S(1)}, u32[]{:S(2)}, u32[]{:S(2)}) %all-to-all-start) | async-done | bytes 2080 | tf_op jit(solution)/shard_map/all_to_all | solution.py:165
  223.1 1.9 gather_fusion.2
  225.0 4.1 %all-to-all-start.1 = ((bf16[32,16,1,128]{3,1,2,0:T(8,128)(2,1)}), bf16[32,16,1,128]{3,1,2,0:T(8,128)(2,1)S(1)}, u32[]{:S(2)}, u32[]{:S(2)}) async-start(bf16[32,16,1,128]{3,1,2,0:T(8,128)(2,1)} %bitcast.36), calls=%async_computation.1 | async-start | bytes 262144 | tf_op jit(solution)/shard_map/all_to_all | solution.py:164
  229.8 10.3 %all-to-all-done.1 = bf16[32,16,1,128]{3,1,2,0:T(8,128)(2,1)S(1)} async-done(((bf16[32,16,1,128]{3,1,2,0:T(8,128)(2,1)}), bf16[32,16,1,128]{3,1,2,0:T(8,128)(2,1)S(1)}, u32[]{:S(2)}, u32[]{:S(2)}) %all-to-all-start.1) | async-done | bytes 131104 | tf_op jit(solution)/shard_map/all_to_all | solution.py:164
  240.1 2.4 scatter_custom_fusion
  242.5 1.1 copy.58
  243.5 1.2 add_convert_fusion
  244.7 0.8 copy.55
  (79 shorter events, 6.8 us)
Async XLA Ops:
  7.2 76.5 %copy-start = (bf16[192,1536]{1,0:T(8,128)(2,1)S(1)}, bf16[192,1536]{1,0:T(8,128)(2,1)}, u32[]{:S(2)}) copy-start(bf16[192,1536]{1,0:T(8,128)(2,1)} %param.24) | copy-start | bytes 1769476
  7.2 57.7 %copy-start.7 = (s32[512]{0:T(512)S(1)}, s32[512]{0:T(512)}, u32[]{:S(2)}) copy-start(s32[512]{0:T(512)} %param.18) | copy-start | bytes 6148
  7.2 57.7 %copy-start.4 = (s32[512]{0:T(512)S(1)}, s32[512]{0:T(512)}, u32[]{:S(2)}) copy-start(s32[512]{0:T(512)} %param.19) | copy-start | bytes 6148
  7.2 60.8 %all-gather.2.cloned.1.call-start = ((), (), s32[]{:S(2)}) async-start(), calls=%async_computation.3 | async-start | bytes 2211840 | tf_op jit(solution)/shard_map/all_gather | solution.py:110
  8.1 22.0 %collective-permute-start = (bf16[48,320]{1,0:T(8,128)(2,1)S(1)}, bf16[48,320]{1,0:T(8,128)(2,1)S(1)}, u32[]{:S(2)}, u32[]{:S(2)}) collective-permute-start(bf16[48,320]{1,0:T(8,128)(2,1)S(1)} %pad_maximum_fusion.3), channel_id=1, source_target_pairs={{0,32},{32,64},{64,96},{96,128},{128,160},{160,192},{192,224},{224... | collective-permute-start | bytes 92168 | tf_op jit(solution)/shard_map/ppermute | solution.py:76
  10.6 21.9 %collective-permute-start.1 = (bf16[48,320]{1,0:T(8,128)(2,1)S(1)}, bf16[48,320]{1,0:T(8,128)(2,1)S(1)}, u32[]{:S(2)}, u32[]{:S(2)}) collective-permute-start(bf16[48,320]{1,0:T(8,128)(2,1)S(1)} %pad_maximum_fusion.3), channel_id=1, source_target_pairs={{0,64},{32,96},{64,128},{96,160},{128,192},{160,224},{192,0},{224,... | collective-permute-start | bytes 92168 | tf_op jit(solution)/shard_map/ppermute | solution.py:76
  13.6 19.8 %collective-permute-start.2 = (bf16[48,320]{1,0:T(8,128)(2,1)S(1)}, bf16[48,320]{1,0:T(8,128)(2,1)S(1)}, u32[]{:S(2)}, u32[]{:S(2)}) collective-permute-start(bf16[48,320]{1,0:T(8,128)(2,1)S(1)} %pad_maximum_fusion.3), channel_id=1, source_target_pairs={{0,96},{32,128},{64,160},{96,192},{128,224},{160,0},{192,32},{224,... | collective-permute-start | bytes 92168 | tf_op jit(solution)/shard_map/ppermute | solution.py:76
  17.4 17.0 %collective-permute-start.3 = (bf16[48,320]{1,0:T(8,128)(2,1)S(1)}, bf16[48,320]{1,0:T(8,128)(2,1)S(1)}, u32[]{:S(2)}, u32[]{:S(2)}) collective-permute-start(bf16[48,320]{1,0:T(8,128)(2,1)S(1)} %pad_maximum_fusion.3), channel_id=1, source_target_pairs={{0,128},{32,160},{64,192},{96,224},{128,0},{160,32},{192,64},{224,... | collective-permute-start | bytes 92168 | tf_op jit(solution)/shard_map/ppermute | solution.py:76
  21.0 157.2 %all-reduce.3.cloned.1.call-start = ((), (), s32[]{:S(2)}) async-start(), calls=%async_computation.4 | async-start | bytes 6291456 | tf_op jit(solution)/shard_map/psum | solution.py:144
  21.1 3.6 %collective-permute-start.10 = (s32[512]{0:T(512)}, s32[512]{0:T(512)S(1)}, u32[]{:S(2)}, u32[]{:S(2)}) collective-permute-start(s32[512]{0:T(512)} %param.18), channel_id=1, source_target_pairs={{0,8},{8,0},{1,9},{9,1},{2,10},{10,2},{3,11},{11,3},{4,12},{12,4},... | collective-permute-start | bytes 6152 | tf_op jit(solution)/shard_map/ppermute | solution.py:132
  24.7 9.7 %collective-permute-start.4 = (bf16[48,320]{1,0:T(8,128)(2,1)S(1)}, bf16[48,320]{1,0:T(8,128)(2,1)S(1)}, u32[]{:S(2)}, u32[]{:S(2)}) collective-permute-start(bf16[48,320]{1,0:T(8,128)(2,1)S(1)} %pad_maximum_fusion.3), channel_id=1, source_target_pairs={{0,160},{32,192},{64,224},{96,0},{128,32},{160,64},{192,96},{224,1... | collective-permute-start | bytes 92168 | tf_op jit(solution)/shard_map/ppermute | solution.py:76
  30.1 4.5 %collective-permute-start.5 = (bf16[48,320]{1,0:T(8,128)(2,1)S(1)}, bf16[48,320]{1,0:T(8,128)(2,1)S(1)}, u32[]{:S(2)}, u32[]{:S(2)}) collective-permute-start(bf16[48,320]{1,0:T(8,128)(2,1)S(1)} %pad_maximum_fusion.3), channel_id=1, source_target_pairs={{0,192},{32,224},{64,0},{96,32},{128,64},{160,96},{192,128},{224,1... | collective-permute-start | bytes 92168 | tf_op jit(solution)/shard_map/ppermute | solution.py:76
  32.6 2.9 %collective-permute-start.6 = (bf16[48,320]{1,0:T(8,128)(2,1)S(1)}, bf16[48,320]{1,0:T(8,128)(2,1)S(1)}, u32[]{:S(2)}, u32[]{:S(2)}) collective-permute-start(bf16[48,320]{1,0:T(8,128)(2,1)S(1)} %pad_maximum_fusion.3), channel_id=1, source_target_pairs={{0,224},{32,0},{64,32},{96,64},{128,96},{160,128},{192,160},{224,1... | collective-permute-start | bytes 92168 | tf_op jit(solution)/shard_map/ppermute | solution.py:76
  33.4 5.8 %collective-permute-start.11 = (s32[512]{0:T(512)}, s32[512]{0:T(512)S(1)}, u32[]{:S(2)}, u32[]{:S(2)}) collective-permute-start(s32[512]{0:T(512)} %param.19), channel_id=1, source_target_pairs={{0,8},{8,0},{1,9},{9,1},{2,10},{10,2},{3,11},{11,3},{4,12},{12,4},... | collective-permute-start | bytes 6152 | tf_op jit(solution)/shard_map/ppermute | solution.py:132
  36.2 27.7 %collective-permute-start.7 = (bf16[8,48,320]{2,1,0:T(8,128)(2,1)S(1)}, bf16[8,48,320]{2,1,0:T(8,128)(2,1)S(1)}, u32[]{:S(2)}, u32[]{:S(2)}) collective-permute-start(bf16[8,48,320]{2,1,0:T(8,128)(2,1)S(1)} %broadcast_select_fusion), channel_id=1, source_target_pairs={{0,16},{16,0},{1,17},{17,1},{2,18},{18,2},{3,19},{19,3},{4,20},{20... | collective-permute-start | bytes 737288 | tf_op jit(solution)/shard_map/ppermute | solution.py:80
  64.1 2.4 collective-permute-start.8
  72.3 4.3 %copy-start.3 = (bf16[8,2,2,48,320]{4,3,2,1,0:T(8,128)(2,1)S(1)}, bf16[8,2,2,48,320]{4,3,2,1,0:T(8,128)(2,1)}, u32[]{:S(2)}) copy-start(bf16[8,2,2,48,320]{4,3,2,1,0:T(8,128)(2,1)} %copy.50) | copy-start | bytes 2949124
  77.5 1.4 collective-permute-start.9
  83.7 2.7 %copy-start.5 = (f32[512,8]{0,1:T(8,128)S(1)}, f32[512,8]{0,1:T(8,128)}, u32[]{:S(2)}) copy-start(f32[512,8]{0,1:T(8,128)} %param.26) | copy-start | bytes 49156
  83.7 2.7 %copy-start.6 = (s32[512,8]{0,1:T(8,128)S(1)}, s32[512,8]{0,1:T(8,128)}, u32[]{:S(2)}) copy-start(s32[512,8]{0,1:T(8,128)} %param.25) | copy-start | bytes 49156
  86.0 156.4 %reduce-scatter.4.cloned.1.call-start = ((), (), s32[]{:S(2)}) async-start(), calls=%async_computation.5 | async-start | bytes 1769472
  180.6 7.6 %copy-start.2 = (bf16[512,1536]{1,0:T(8,128)(2,1)}, bf16[512,1536]{1,0:T(8,128)(2,1)S(1)}, u32[]{:S(2)}) copy-start(bf16[512,1536]{1,0:T(8,128)(2,1)S(1)} %get-tuple-element.47) | copy-start | bytes 4718596
  180.6 7.6 %copy-start.8 = (bf16[5,256,1536]{2,1,0:T(8,128)(2,1)S(1)}, bf16[5,256,1536]{2,1,0:T(8,128)(2,1)}, u32[]{:S(2)}) copy-start(bf16[5,256,1536]{2,1,0:T(8,128)(2,1)} %param.28) | copy-start | bytes 11796484
  191.7 1.6 copy-start.1
  201.3 21.6 %all-to-all-start = ((s32[32,1,16]{2,1,0:T(1,128)}), s32[32,1,16]{2,1,0:T(1,128)S(1)}, u32[]{:S(2)}, u32[]{:S(2)}) async-start(s32[32,1,16]{2,1,0:T(1,128)} %bitcast.32), calls=%async_computation | async-start | bytes 32768 | tf_op jit(solution)/shard_map/all_to_all | solution.py:165
  225.0 15.1 %all-to-all-start.1 = ((bf16[32,16,1,128]{3,1,2,0:T(8,128)(2,1)}), bf16[32,16,1,128]{3,1,2,0:T(8,128)(2,1)S(1)}, u32[]{:S(2)}, u32[]{:S(2)}) async-start(bf16[32,16,1,128]{3,1,2,0:T(8,128)(2,1)} %bitcast.36), calls=%async_computation.1 | async-start | bytes 262144 | tf_op jit(solution)/shard_map/all_to_all | solution.py:164
Sparse Core Ops, SparseCore 0:
  21.1 40.3 all-gather.1
  86.2 91.9 all-reduce.2
  193.4 40.6 reduce-scatter.3
where the time goes:
time: 253 us; the launch traced here: 252 us
  waiting for transfers between devices  138 us (55%)
  starting transfers between devices  41.3 us (16%)
  local copies, waits for them, and re-layouts  19.8 us (8%)
  other arithmetic  19.5 us (8%)
  matrix products  19.4 us (8%)
  between operations  14.2 us (6%)
    psum x1, waiting for transfers between devices, shards(): summed = lax.psum(partial_value, T)  91.7 us
    ppermute x1, waiting for transfers between devices, gather_rows_over_groups(): other_y = lax.ppermute(zfull, 'yh', [(0, 1), (1, 0)])  23.9 us
    ppermute x7, starting transfers between devices, gather_rows_over_groups(): got.append(lax.ppermute(block, 'z', [(i, (i + k) % nz) for i in range(nz)]))  17.7 us
    all_to_all x1, starting transfers between devices, shards(): lax.all_to_all(send_slots, G, split_axis=0, concat_axis=0, tiled=True)  12.2 us
    all_to_all x1, waiting for transfers between devices, shards(): lax.all_to_all(send_rows, G, split_axis=0, concat_axis=0, tiled=True)  10.3 us
    all_to_all x1, waiting for transfers between devices, shards(): lax.all_to_all(send_slots, G, split_axis=0, concat_axis=0, tiled=True)  9.3 us
    dot_general x1, matrix products, expert_terms(): jnp.einsum('td,edf->etf', normed, gateup, preferred_element_type=jnp.floa...  7.52 us
    unnamed x28, local copies, waits for them, and re-layouts  5.28 us
  transfers between devices with their start and end apart: 17, of which 8 were waited for; matrix products, arithmetic and copies ran while one was open for 9% of the time, Pallas kernels for 0%

commit v1 on v0

--- a/solution.py
+++ b/solution.py
@@ -141,7 +141,8 @@
     attended = mixed.reshape(tokens, heads_local * HD)
     log_sums = log_part.reshape(heads_local, tokens)
     partial_value = jnp.dot(attended, output_weight, preferred_element_type=jnp.float32)
-    summed = lax.psum(partial_value, T)
+    inner = lax.psum(partial_value, "yl")
+    summed = lax.psum(inner, "x")
     residual = (states_full.astype(jnp.float32) + summed).astype(jnp.bfloat16)
     normed = rms_scale(residual, gain_forward)
     residual_share = lax.dynamic_slice_in_dim(residual, head_rank * width_share, width_share, 1)

time: 253 us -> 339 us (1.34)
  waiting for transfers between devices: 138 us -> 226 us
    psum x1 -> x2, waiting for transfers between devices: 91.7 us -> 180 us  [the longest x1 96.2 us: shards(): inner = lax.psum(partial_value, 'yl')]
  transfers between devices with their start and end apart: 17 -> 18, of which waited for: 8 -> 9; matrix products, arithmetic and copies ran while one was open for 9% -> 7% of each run, Pallas kernels for 0% -> 0%
where the time goes in v1:
time: 339 us
  waiting for transfers between devices  226 us (67%)
  starting transfers between devices  39.3 us (12%)
  local copies, waits for them, and re-layouts  19.8 us (6%)
  other arithmetic  19.5 us (6%)
  matrix products  19.4 us (6%)
  between operations  14.2 us (4%)
    psum x1, waiting for transfers between devices, shards(): inner = lax.psum(partial_value, 'yl')  96.2 us
    psum x1, waiting for transfers between devices, shards(): summed = lax.psum(inner, 'x')  83.9 us
    ppermute x1, waiting for transfers between devices, gather_rows_over_groups(): other_y = lax.ppermute(zfull, 'yh', [(0, 1), (1, 0)])  23.9 us
    ppermute x7, starting transfers between devices, gather_rows_over_groups(): got.append(lax.ppermute(block, 'z', [(i, (i + k) % nz) for i in range(nz)]))  17.7 us
    all_to_all x1, waiting for transfers between devices, shards(): lax.all_to_all(send_rows, G, split_axis=0, concat_axis=0, tiled=True)  10.3 us
    all_to_all x1, starting transfers between devices, shards(): lax.all_to_all(send_slots, G, split_axis=0, concat_axis=0, tiled=True)  10.3 us
    all_to_all x1, waiting for transfers between devices, shards(): lax.all_to_all(send_slots, G, split_axis=0, concat_axis=0, tiled=True)  9.28 us
    dot_general x1, matrix products, expert_terms(): jnp.einsum('td,edf->etf', normed, gateup, preferred_element_type=jnp.floa...  7.52 us
  transfers between devices with their start and end apart: 18, of which 9 were waited for; matrix products, arithmetic and copies ran while one was open for 7% of the time, Pallas kernels for 0%

profile of v1, /device:TPU:1, one launch (start us, length us, event | category | flops | bytes accessed | tf_op | source)
XLA Modules:
  0.0 338.6 jit_solution(17400424234452786698)
XLA Ops:
  7.2 0.9 pad_maximum_fusion.3
  8.1 2.5 collective-permute-start
  10.6 3.0 collective-permute-start.1
  13.6 3.8 %collective-permute-start.2 = (bf16[48,320]{1,0:T(8,128)(2,1)S(1)}, bf16[48,320]{1,0:T(8,128)(2,1)S(1)}, u32[]{:S(2)}, u32[]{:S(2)}) collective-permute-start(bf16[48,320]{1,0:T(8,128)(2,1)S(1)} %pad_maximum_fusion.3), channel_id=1, source_target_pairs={{0,96},{32,128},{64,160},{96,192},{128,224},{160,0},{192,32},{224,... | collective-permute-start | bytes 92168 | tf_op jit(solution)/shard_map/ppermute | solution.py:76
  19.3 1.7 pad_maximum_fusion.1
  21.1 1.7 collective-permute-start.10
  22.7 0.8 bitcast_dynamic-update-slice_fusion.7
  23.6 0.7 convert_element_type.66
  24.7 4.7 %collective-permute-start.4 = (bf16[48,320]{1,0:T(8,128)(2,1)S(1)}, bf16[48,320]{1,0:T(8,128)(2,1)S(1)}, u32[]{:S(2)}, u32[]{:S(2)}) collective-permute-start(bf16[48,320]{1,0:T(8,128)(2,1)S(1)} %pad_maximum_fusion.3), channel_id=1, source_target_pairs={{0,160},{32,192},{64,224},{96,0},{128,32},{160,64},{192,96},{224,1... | collective-permute-start | bytes 92168 | tf_op jit(solution)/shard_map/ppermute | solution.py:76
  29.4 0.7 pad_add_fusion
  30.1 2.5 collective-permute-start.5
  32.6 0.8 collective-permute-start.6
  33.4 0.9 collective-permute-start.11
  34.6 0.8 collective-permute-done.6
  36.2 3.0 collective-permute-start.7
  39.2 0.7 pad_add_fusion.1
  40.0 23.9 %collective-permute-done.7 = bf16[8,48,320]{2,1,0:T(8,128)(2,1)S(1)} collective-permute-done((bf16[8,48,320]{2,1,0:T(8,128)(2,1)S(1)}, bf16[8,48,320]{2,1,0:T(8,128)(2,1)S(1)}, u32[]{:S(2)}, u32[]{:S(2)}) %collective-permute-start.7) | collective-permute-done | bytes 245792 | tf_op jit(solution)/shard_map/ppermute | solution.py:80
  64.1 0.8 collective-permute-start.8
  64.8 0.8 compare_and_fusion
  66.8 1.1 copy.50
  68.0 2.6 slice.95
  70.6 1.7 copy.59
  72.7 1.5 convert_reduce_fusion
  74.3 2.0 convolution_bitcast_fusion.1
  76.6 0.8 fusion.22
  78.0 0.9 collective-permute-done.9
  78.9 1.3 fusion.1
  80.2 1.4 fusion
  81.6 2.0 fusion.19
  83.7 2.3 fusion.54
  86.1 96.2 %all-reduce.4.cloned.1.call-done = f32[512,1536]{1,0:T(8,128)} async-done(((f32[512,1536]{1,0:T(8,128)}), f32[512,1536]{1,0:T(8,128)}) %all-reduce.4.cloned.1.call-update) | async-done | bytes 3145744 | tf_op jit(solution)/shard_map/psum | solution.py:144
  182.7 83.9 %all-reduce.6.cloned.1.call-done = f32[512,1536]{1,0:T(8,128)} async-done(((f32[512,1536]{1,0:T(8,128)}), f32[512,1536]{1,0:T(8,128)}) %all-reduce.6.cloned.1.call-update) | async-done | bytes 3145744 | tf_op jit(solution)/shard_map/psum | solution.py:145
  266.7 2.4 fusion.2
  269.1 7.5 %convolution_bitcast_fusion = f32[5,512,512]{2,1,0:T(8,128)S(1)} fusion(bf16[5,1536,512]{2,1,0:T(8,128)(2,1)} %param.27, bf16[512,1536]{1,0:T(8,128)(2,1)S(1)} %get-tuple-element.47, f32[1536]{0:T(1024)S(1)} %get-tuple-element.44, f32[512]{0:T(512)S(1)} %add_rsqrt_fusion), kind=kOutput, calls=%fused_computation.26 | convolution fusion | flops 4029677568 | bytes 14688256 | tf_op jit(solution)/shard_map/td,edf->etf/dot_general | solution.py:62
  276.7 3.5 %multiply_reduce_fusion = bf16[512,1536]{1,0:T(8,128)(2,1)S(1)} fusion(bf16[5,256,1536]{2,1,0:T(8,128)(2,1)S(1)} %copy-done.8, f32[5,512]{1,0:T(8,128)S(1)} %bitcast.103, f32[5,512,512]{2,1,0:T(8,128)S(1)} %convolution_bitcast_fusion), kind=kOutput, calls=%fused_computation.4 | convolution fusion | flops 2024275968 | bytes 10758144 | tf_op jit(solution)/shard_map/etf,efd->etd/dot_general | solution.py:66
  280.2 1.6 copy.57
  281.8 3.8 %sort.17 = (s32[512]{0:T(512)}, s32[512]{0:T(512)S(1)}) sort(s32[512]{0:T(512)S(1)} %fusion.43, s32[512]{0:T(512)S(1)} %iota.31), dimensions={0}, to_apply=%region_9.10 | sort | flops 4608 | bytes 8192 | tf_op jit(solution)/shard_map/jit(argsort)/sort | solution.py:161
  285.6 3.5 %gather_fusion.1 = s32[512]{0:T(512)S(1)} fusion(s32[512]{0:T(512)S(1)} %copy-done.1, s32[1024]{0:T(1024)S(1)} %pad_clamp_fusion), kind=kCustom, calls=%fused_computation.1 | custom fusion | bytes 6144 | tf_op jit(solution)/shard_map/gather | solution.py:163
  289.1 0.7 all_to_all.9
  289.8 10.3 %all-to-all-start = ((s32[32,1,16]{2,1,0:T(1,128)}), s32[32,1,16]{2,1,0:T(1,128)S(1)}, u32[]{:S(2)}, u32[]{:S(2)}) async-start(s32[32,1,16]{2,1,0:T(1,128)} %bitcast.32), calls=%async_computation | async-start | bytes 32768 | tf_op jit(solution)/shard_map/all_to_all | solution.py:166
  300.1 9.3 %all-to-all-done = s32[32,1,16]{2,1,0:T(1,128)S(1)} async-done(((s32[32,1,16]{2,1,0:T(1,128)}), s32[32,1,16]{2,1,0:T(1,128)S(1)}, u32[]{:S(2)}, u32[]{:S(2)}) %all-to-all-start) | async-done | bytes 2080 | tf_op jit(solution)/shard_map/all_to_all | solution.py:166
  309.6 1.9 gather_fusion.2
  311.5 4.1 %all-to-all-start.1 = ((bf16[32,16,1,128]{3,1,2,0:T(8,128)(2,1)}), bf16[32,16,1,128]{3,1,2,0:T(8,128)(2,1)S(1)}, u32[]{:S(2)}, u32[]{:S(2)}) async-start(bf16[32,16,1,128]{3,1,2,0:T(8,128)(2,1)} %bitcast.36), calls=%async_computation.1 | async-start | bytes 262144 | tf_op jit(solution)/shard_map/all_to_all | solution.py:165
  316.3 10.3 %all-to-all-done.1 = bf16[32,16,1,128]{3,1,2,0:T(8,128)(2,1)S(1)} async-done(((bf16[32,16,1,128]{3,1,2,0:T(8,128)(2,1)}), bf16[32,16,1,128]{3,1,2,0:T(8,128)(2,1)S(1)}, u32[]{:S(2)}, u32[]{:S(2)}) %all-to-all-start.1) | async-done | bytes 131104 | tf_op jit(solution)/shard_map/all_to_all | solution.py:165
  326.6 2.4 scatter_custom_fusion
  329.0 1.1 copy.58
  330.1 1.2 add_convert_fusion
  331.2 0.8 copy.55
  (82 shorter events, 7.5 us)
Async XLA Ops:
  7.2 76.5 %copy-start = (bf16[192,1536]{1,0:T(8,128)(2,1)S(1)}, bf16[192,1536]{1,0:T(8,128)(2,1)}, u32[]{:S(2)}) copy-start(bf16[192,1536]{1,0:T(8,128)(2,1)} %param.24) | copy-start | bytes 1769476
  7.2 57.7 %copy-start.7 = (s32[512]{0:T(512)S(1)}, s32[512]{0:T(512)}, u32[]{:S(2)}) copy-start(s32[512]{0:T(512)} %param.18) | copy-start | bytes 6148
  7.2 57.7 %copy-start.4 = (s32[512]{0:T(512)S(1)}, s32[512]{0:T(512)}, u32[]{:S(2)}) copy-start(s32[512]{0:T(512)} %param.19) | copy-start | bytes 6148
  7.2 60.8 %all-gather.2.cloned.1.call-start = ((), (), s32[]{:S(2)}) async-start(), calls=%async_computation.3 | async-start | bytes 2211840 | tf_op jit(solution)/shard_map/all_gather | solution.py:110
  8.1 22.0 %collective-permute-start = (bf16[48,320]{1,0:T(8,128)(2,1)S(1)}, bf16[48,320]{1,0:T(8,128)(2,1)S(1)}, u32[]{:S(2)}, u32[]{:S(2)}) collective-permute-start(bf16[48,320]{1,0:T(8,128)(2,1)S(1)} %pad_maximum_fusion.3), channel_id=1, source_target_pairs={{0,32},{32,64},{64,96},{96,128},{128,160},{160,192},{192,224},{224... | collective-permute-start | bytes 92168 | tf_op jit(solution)/shard_map/ppermute | solution.py:76
  10.6 21.9 %collective-permute-start.1 = (bf16[48,320]{1,0:T(8,128)(2,1)S(1)}, bf16[48,320]{1,0:T(8,128)(2,1)S(1)}, u32[]{:S(2)}, u32[]{:S(2)}) collective-permute-start(bf16[48,320]{1,0:T(8,128)(2,1)S(1)} %pad_maximum_fusion.3), channel_id=1, source_target_pairs={{0,64},{32,96},{64,128},{96,160},{128,192},{160,224},{192,0},{224,... | collective-permute-start | bytes 92168 | tf_op jit(solution)/shard_map/ppermute | solution.py:76
  13.6 19.8 %collective-permute-start.2 = (bf16[48,320]{1,0:T(8,128)(2,1)S(1)}, bf16[48,320]{1,0:T(8,128)(2,1)S(1)}, u32[]{:S(2)}, u32[]{:S(2)}) collective-permute-start(bf16[48,320]{1,0:T(8,128)(2,1)S(1)} %pad_maximum_fusion.3), channel_id=1, source_target_pairs={{0,96},{32,128},{64,160},{96,192},{128,224},{160,0},{192,32},{224,... | collective-permute-start | bytes 92168 | tf_op jit(solution)/shard_map/ppermute | solution.py:76
  17.4 17.0 %collective-permute-start.3 = (bf16[48,320]{1,0:T(8,128)(2,1)S(1)}, bf16[48,320]{1,0:T(8,128)(2,1)S(1)}, u32[]{:S(2)}, u32[]{:S(2)}) collective-permute-start(bf16[48,320]{1,0:T(8,128)(2,1)S(1)} %pad_maximum_fusion.3), channel_id=1, source_target_pairs={{0,128},{32,160},{64,192},{96,224},{128,0},{160,32},{192,64},{224,... | collective-permute-start | bytes 92168 | tf_op jit(solution)/shard_map/ppermute | solution.py:76
  21.0 161.3 %all-reduce.4.cloned.1.call-start = ((), (), s32[]{:S(2)}) async-start(), calls=%async_computation.4 | async-start | bytes 6291456 | tf_op jit(solution)/shard_map/psum | solution.py:144
  21.1 3.6 %collective-permute-start.10 = (s32[512]{0:T(512)}, s32[512]{0:T(512)S(1)}, u32[]{:S(2)}, u32[]{:S(2)}) collective-permute-start(s32[512]{0:T(512)} %param.18), channel_id=1, source_target_pairs={{0,8},{8,0},{1,9},{9,1},{2,10},{10,2},{3,11},{11,3},{4,12},{12,4},... | collective-permute-start | bytes 6152 | tf_op jit(solution)/shard_map/ppermute | solution.py:132
  24.7 9.7 %collective-permute-start.4 = (bf16[48,320]{1,0:T(8,128)(2,1)S(1)}, bf16[48,320]{1,0:T(8,128)(2,1)S(1)}, u32[]{:S(2)}, u32[]{:S(2)}) collective-permute-start(bf16[48,320]{1,0:T(8,128)(2,1)S(1)} %pad_maximum_fusion.3), channel_id=1, source_target_pairs={{0,160},{32,192},{64,224},{96,0},{128,32},{160,64},{192,96},{224,1... | collective-permute-start | bytes 92168 | tf_op jit(solution)/shard_map/ppermute | solution.py:76
  30.1 4.5 %collective-permute-start.5 = (bf16[48,320]{1,0:T(8,128)(2,1)S(1)}, bf16[48,320]{1,0:T(8,128)(2,1)S(1)}, u32[]{:S(2)}, u32[]{:S(2)}) collective-permute-start(bf16[48,320]{1,0:T(8,128)(2,1)S(1)} %pad_maximum_fusion.3), channel_id=1, source_target_pairs={{0,192},{32,224},{64,0},{96,32},{128,64},{160,96},{192,128},{224,1... | collective-permute-start | bytes 92168 | tf_op jit(solution)/shard_map/ppermute | solution.py:76
  32.6 2.9 collective-permute-start.6
  33.4 5.8 %collective-permute-start.11 = (s32[512]{0:T(512)}, s32[512]{0:T(512)S(1)}, u32[]{:S(2)}, u32[]{:S(2)}) collective-permute-start(s32[512]{0:T(512)} %param.19), channel_id=1, source_target_pairs={{0,8},{8,0},{1,9},{9,1},{2,10},{10,2},{3,11},{11,3},{4,12},{12,4},... | collective-permute-start | bytes 6152 | tf_op jit(solution)/shard_map/ppermute | solution.py:132
  36.2 27.7 %collective-permute-start.7 = (bf16[8,48,320]{2,1,0:T(8,128)(2,1)S(1)}, bf16[8,48,320]{2,1,0:T(8,128)(2,1)S(1)}, u32[]{:S(2)}, u32[]{:S(2)}) collective-permute-start(bf16[8,48,320]{2,1,0:T(8,128)(2,1)S(1)} %broadcast_select_fusion), channel_id=1, source_target_pairs={{0,16},{16,0},{1,17},{17,1},{2,18},{18,2},{3,19},{19,3},{4,20},{20... | collective-permute-start | bytes 737288 | tf_op jit(solution)/shard_map/ppermute | solution.py:80
  64.1 2.4 collective-permute-start.8
  72.3 4.3 %copy-start.3 = (bf16[8,2,2,48,320]{4,3,2,1,0:T(8,128)(2,1)S(1)}, bf16[8,2,2,48,320]{4,3,2,1,0:T(8,128)(2,1)}, u32[]{:S(2)}) copy-start(bf16[8,2,2,48,320]{4,3,2,1,0:T(8,128)(2,1)} %copy.50) | copy-start | bytes 2949124
  77.5 1.4 collective-permute-start.9
  86.0 96.6 %copy-start.5 = (f32[512,8]{0,1:T(8,128)S(1)}, f32[512,8]{0,1:T(8,128)}, u32[]{:S(2)}) copy-start(f32[512,8]{0,1:T(8,128)} %param.26) | copy-start | bytes 49156
  86.0 96.6 %copy-start.6 = (s32[512,8]{0,1:T(8,128)S(1)}, s32[512,8]{0,1:T(8,128)}, u32[]{:S(2)}) copy-start(s32[512,8]{0,1:T(8,128)} %param.25) | copy-start | bytes 49156
  86.0 180.6 %all-reduce.6.cloned.1.call-start = ((), (), s32[]{:S(2)}) async-start(), calls=%async_computation.5 | async-start | bytes 6291456 | tf_op jit(solution)/shard_map/psum | solution.py:145
  182.3 146.7 %reduce-scatter.4.cloned.1.call-start = ((), (), s32[]{:S(2)}) async-start(), calls=%async_computation.6 | async-start | bytes 1769472
  269.1 7.6 %copy-start.2 = (bf16[512,1536]{1,0:T(8,128)(2,1)}, bf16[512,1536]{1,0:T(8,128)(2,1)S(1)}, u32[]{:S(2)}) copy-start(bf16[512,1536]{1,0:T(8,128)(2,1)S(1)} %get-tuple-element.47) | copy-start | bytes 4718596
  269.1 7.6 %copy-start.8 = (bf16[5,256,1536]{2,1,0:T(8,128)(2,1)S(1)}, bf16[5,256,1536]{2,1,0:T(8,128)(2,1)}, u32[]{:S(2)}) copy-start(bf16[5,256,1536]{2,1,0:T(8,128)(2,1)} %param.28) | copy-start | bytes 11796484
  280.1 1.6 copy-start.1
  289.8 19.6 %all-to-all-start = ((s32[32,1,16]{2,1,0:T(1,128)}), s32[32,1,16]{2,1,0:T(1,128)S(1)}, u32[]{:S(2)}, u32[]{:S(2)}) async-start(s32[32,1,16]{2,1,0:T(1,128)} %bitcast.32), calls=%async_computation | async-start | bytes 32768 | tf_op jit(solution)/shard_map/all_to_all | solution.py:166
  311.5 15.1 %all-to-all-start.1 = ((bf16[32,16,1,128]{3,1,2,0:T(8,128)(2,1)}), bf16[32,16,1,128]{3,1,2,0:T(8,128)(2,1)S(1)}, u32[]{:S(2)}, u32[]{:S(2)}) async-start(bf16[32,16,1,128]{3,1,2,0:T(8,128)(2,1)} %bitcast.36), calls=%async_computation.1 | async-start | bytes 262144 | tf_op jit(solution)/shard_map/all_to_all | solution.py:165
Sparse Core Ops, SparseCore 0:
  21.1 40.3 all-gather.1
  86.1 96.1 all-reduce.3
  184.8 81.8 all-reduce.5
  281.9 38.3 reduce-scatter.3
